TPU v7x, 256 devices: a whole 4x4x8 slice. The times are simulated.
256 devices in a mesh: tm: 32 (over y, x, core), tensor: 8 (over z).
Axes of the slice: x: 4, y: 4, z: 8, core: 2. Of those that a mesh axis runs over, the one named last changes fastest.
Arguments:
- features: bfloat16 [32768, 1536], P(('tm', 'tensor')), may hold values from -4 to 4
- frame_mask: int32 [32768], P('tm'), may hold values 0 or 1
- total_length: int32 [1], replicated, may hold values from 24576 to 32768
- norm_gain: float32 [1536], replicated, may hold values from 0.1 to 1.9
- value_weight: bfloat16 [1536, 1536], P(None, 'tensor'), may hold values from -0.15625 to 0.15625
- gate_weight: bfloat16 [1536, 1536], P(None, 'tensor'), may hold values from -0.15625 to 0.15625
- depth_kernel: float32 [31, 1536], P(None, 'tensor'), may hold values from -1 to 1
- batch_gain: float32 [1536], P('tensor'), may hold values from 0.1 to 1.9
- batch_bias: float32 [1536], P('tensor'), may hold values from -2 to 2
- out_weight: bfloat16 [1536, 1536], P('tensor'), may hold values from -0.15625 to 0.15625
- feed_gain: float32 [1536], replicated, may hold values from 0.1 to 1.9
- up_weight: bfloat16 [1536, 6144], P('tm', 'tensor'), may hold values from -0.15625 to 0.15625
- down_weight: bfloat16 [6144, 1536], P('tensor', 'tm'), may hold values from -0.078125 to 0.078125
Outputs:
- encoded: bfloat16 [32768, 1536], P(('tm', 'tensor'))
All inputs are finite; a program needn't handle non-finite values. No bound on the sum of `frame_mask` on one device may be relied on, other than what follows from the above.
Results may differ from a plain program's by a relative error of at most 0.0074.
Values may be sent and summed in bfloat16 or wider, within the bound.
No kernel may reach another device: no remote copies, remote signals or barrier semaphores. Data moves between devices by JAX's collectives and lax.ppermute only.
A program may use at most 64 MiB of HBM per device.

v0:
```python
import jax
import jax.numpy as jnp
from jax import lax
from jax.sharding import PartitionSpec as P

KERNEL = 31


def extended(array, sides, width):
    for axis, dim in sides:
        devices, length = (lax.axis_size(axis), array.shape[dim])
        up = [(i, (i + 1) % devices) for i in range(devices - 1)]
        down = [(j, i) for i, j in up]
        last = lax.slice_in_dim(array, length - width, length, axis=dim)
        initial = lax.slice_in_dim(array, 0, width, axis=dim)
        before = lax.ppermute(last, axis, up)
        after = lax.ppermute(initial, axis, down)
        array = jnp.concatenate([before, array, after], axis=dim)
    return array


def layer_norm(rows, gain):
    values = rows.astype(jnp.float32)
    centre = jnp.mean(values, axis=-1, keepdims=True)
    spread = jnp.mean(jnp.square(values - centre), axis=-1, keepdims=True)
    return (values - centre) * lax.rsqrt(spread + 1e-05) * gain


def shards(
    features,
    frame_mask,
    total_length,
    norm_gain,
    value_weight,
    gate_weight,
    depth_kernel,
    batch_gain,
    batch_bias,
    out_weight,
    feed_gain,
    up_weight,
    down_weight,
):
    own_rows = features.shape[0]
    block = own_rows * lax.axis_size("tensor")
    positions = lax.axis_index("tm") * block + jnp.arange(block, dtype=jnp.int32)
    valid = ((frame_mask > 0) & (positions < total_length[0])).astype(jnp.float32)
    normed = layer_norm(features, norm_gain).astype(jnp.bfloat16)
    piece = lax.all_gather(normed, "tensor", axis=0, tiled=True)
    value = jnp.dot(piece, value_weight, preferred_element_type=jnp.float32)
    gate = jnp.dot(piece, gate_weight, preferred_element_type=jnp.float32)
    glu = (value * jax.nn.sigmoid(gate) * valid[:, None]).astype(jnp.bfloat16)
    padded = extended(glu, (("tm", 0),), KERNEL // 2)
    conv = jnp.zeros(glu.shape, jnp.float32)
    for tap in range(KERNEL):
        conv = conv + padded[tap : tap + block].astype(jnp.float32) * depth_kernel[tap]
    count_local = jnp.sum(valid)
    first_sum = jnp.sum(conv * valid[:, None], axis=0)
    total, count = lax.psum((first_sum, count_local), "tm")
    mean = total / count
    centred = conv - mean
    spread = lax.psum(jnp.sum(jnp.square(centred) * valid[:, None], axis=0), "tm")
    var = spread / count
    scaled = centred * lax.rsqrt(var + 1e-05) * batch_gain + batch_bias
    swished = (scaled * jax.nn.sigmoid(scaled)).astype(jnp.bfloat16)
    conv_out = lax.psum_scatter(
        jnp.dot(swished, out_weight, preferred_element_type=jnp.float32),
        "tensor",
        scatter_dimension=0,
        tiled=True,
    )
    mid = (features.astype(jnp.float32) + conv_out).astype(jnp.bfloat16)
    feed_normed = layer_norm(mid, feed_gain).astype(jnp.bfloat16)
    feed_block = lax.all_gather(feed_normed, "tensor", axis=0, tiled=True)
    up_whole = lax.all_gather(up_weight, "tm", axis=0, tiled=True)
    pre = jnp.dot(feed_block, up_whole, preferred_element_type=jnp.float32)
    hidden = (pre * jax.nn.sigmoid(pre)).astype(jnp.bfloat16)
    down_whole = lax.all_gather(down_weight, "tm", axis=1, tiled=True)
    partial_out = jnp.dot(hidden, down_whole, preferred_element_type=jnp.float32)
    feed_out = lax.psum_scatter(partial_out, "tensor", scatter_dimension=0, tiled=True)
    return (mid.astype(jnp.float32) + 0.5 * feed_out).astype(jnp.bfloat16)


def solution(mesh):
    placed = (
        P(("tm", "tensor"), None),
        P("tm"),
        P(),
        P(),
        P(None, "tensor"),
        P(None, "tensor"),
        P(None, "tensor"),
        P("tensor"),
        P("tensor"),
        P("tensor", None),
        P(),
        P("tm", "tensor"),
        P("tensor", "tm"),
    )
    return jax.shard_map(
        shards, mesh=mesh, in_specs=placed, out_specs=P(("tm", "tensor"), None), check_vma=False
    )
```

profile of v0, /device:TPU:1, one launch (start us, length us, event | category | flops | bytes accessed | tf_op | source)
XLA Modules:
  0.0 450.7 jit_solution(13662535378616291768)
XLA Ops:
  7.4 1.2 convert_reduce_fusion.1
  8.6 1.2 fusion.14
  9.8 2.0 fusion.16
  12.6 1.4 fusion.58
  14.0 1.0 fusion.61
  15.0 45.6 %all-gather.5.cloned.1.call-done = bf16[1024,1536]{1,0:T(8,128)(2,1)} async-done(((bf16[128,1536]{1,0:T(8,128)(2,1)}), bf16[1024,1536]{1,0:T(8,128)(2,1)}) %all-gather.5.cloned.1.call-update) | async-done | bytes 3145744 | tf_op jit(solution)/shard_map/all_gather | solution.py:49
  60.6 3.4 fusion.5
  64.0 1.2 fusion.6
  65.3 3.9 collective-permute-start
  69.2 1.9 collective-permute-start.1
  71.1 1.0 fusion.62
  72.1 2.5 collective-permute-done.1
  74.6 5.6 %multiply_reduce_fusion.1 = (f32[192]{0:T(256)S(1)}, f32[1024,192]{0,1:T(8,128)S(1)}) fusion(f32[1024]{0:T(1024)S(1)} %get-tuple-element.10, f32[192]{0:T(256)S(1)} %bitcast.70, bf16[15,192]{0,1:T(8,128)(2,1)S(1)} %collective-permute-done.1, bf16[1024,192]{0,1:T(8,128)(2,1)S(1)} %fusion.6, f32[192]{0:T(256)S(1)} %bitcast.71, f32[192]{0:T(256)S(1)} %bitcast.42, ...), kind=kLoop, calls=%fused_computation.58 | loop fusion | flops 36175680 | bytes 1219840 | tf_op jit(solution)/shard_map/reduce_sum | solution.py:58
  80.2 61.4 %all-reduce = (f32[192]{0:T(256)S(1)}, f32[]{:T(128)}) all-reduce(f32[192]{0:T(256)S(1)} %get-tuple-element.11, f32[]{:T(128)} %get-tuple-element.9), channel_id=1, replica_groups=mesh['tm'=32,'tensor'=8] {'tm'}, use_global_device_ids=true, to_apply=%region_3.0 | all-reduce | flops 193 | bytes 1544 | tf_op jit(solution)/shard_map/psum | solution.py:59
  142.5 65.3 %psum.23 = f32[192]{0:T(256)S(1)} all-reduce(f32[192]{0:T(256)S(1)} %multiply_reduce_fusion), channel_id=1, replica_groups=mesh['tm'=32,'tensor'=8] {'tm'}, use_global_device_ids=true, to_apply=%region_7.0 | all-reduce | flops 192 | bytes 1536 | tf_op jit(solution)/shard_map/psum | solution.py:62
  208.4 3.9 fusion.19
  213.6 67.8 %reduce-scatter.3.cloned.1.call-done = f32[128,1536]{1,0:T(8,128)} async-done(((f32[1024,1536]{1,0:T(8,128)}), f32[128,1536]{1,0:T(8,128)}) %reduce-scatter.3.cloned.1.call-update) | async-done | bytes 786448 | tf_op jit(solution)/shard_map/reduce_scatter | solution.py:66
  281.4 1.3 convert_reduce_fusion
  283.0 1.0 fusion.13
  284.3 25.3 %all-gather.11.cloned.1.call-done = bf16[768,1536]{0,1:T(8,128)(2,1)} async-done(((bf16[768,48]{0,1:T(8,128)(2,1)}), bf16[768,1536]{0,1:T(8,128)(2,1)}) %all-gather.11.cloned.1.call-update) | async-done | bytes 2359312 | tf_op jit(solution)/shard_map/all_gather | solution.py:78
  309.6 45.3 %all-gather.7.cloned.1.call-done = bf16[1024,1536]{1,0:T(8,128)(2,1)} async-done(((bf16[128,1536]{1,0:T(8,128)(2,1)}), bf16[1024,1536]{1,0:T(8,128)(2,1)}) %all-gather.7.cloned.1.call-update) | async-done | bytes 3145744 | tf_op jit(solution)/shard_map/all_gather | solution.py:74
  354.9 12.1 %fusion = f32[1024,1536]{1,0:T(8,128)} fusion(bf16[768,1536]{0,1:T(8,128)(2,1)} %all-gather.11.cloned.1.call-done, bf16[1024,1536]{1,0:T(8,128)(2,1)} %all-gather.7.cloned.1.call-done, bf16[1536,768]{1,0:T(8,128)(2,1)} %all-gather.9.cloned.1.call-done), kind=kOutput, calls=%fused_computation.29 | convolution fusion | flops 4835770368 | bytes 14155776 | tf_op jit(solution)/shard_map/dot_general | solution.py:79
  367.0 74.2 %reduce-scatter.5.cloned.1.call-done = f32[128,1536]{1,0:T(8,128)} async-done(((f32[1024,1536]{1,0:T(8,128)}), f32[128,1536]{1,0:T(8,128)}) %reduce-scatter.5.cloned.1.call-update) | async-done | bytes 786448 | tf_op jit(solution)/shard_map/reduce_scatter | solution.py:80
  441.2 2.0 fusion.18
  (37 shorter events, 3.5 us)
Async XLA Ops:
  7.4 201.1 %copy-start = (bf16[192,1536]{1,0:T(8,128)(2,1)S(1)}, bf16[192,1536]{1,0:T(8,128)(2,1)}, u32[]{:S(2)}) copy-start(bf16[192,1536]{1,0:T(8,128)(2,1)} %param.22) | copy-start | bytes 1769476
  7.4 53.2 %all-gather.5.cloned.1.call-start = ((), (), s32[]{:S(2)}) async-start(), calls=%async_computation.2 | async-start | bytes 3538944 | tf_op jit(solution)/shard_map/all_gather | solution.py:49
  11.9 269.5 %reduce-scatter.3.cloned.1.call-start = ((), (), s32[]{:S(2)}) async-start(), calls=%async_computation.3 | async-start | bytes 7077888 | tf_op jit(solution)/shard_map/reduce_scatter | solution.py:66
  15.0 49.0 %copy-start.6 = (bf16[1536,192]{0,1:T(8,128)(2,1)S(1)}, bf16[1536,192]{0,1:T(8,128)(2,1)}, u32[]{:S(2)}) copy-start(bf16[1536,192]{0,1:T(8,128)(2,1)} %param.17) | copy-start | bytes 1769476
  60.6 3.4 copy-start.5
  64.0 144.4 %copy-start.3 = (f32[192]{0:T(256)S(1)}, f32[192]{0:T(256)}, u32[]{:S(2)}) copy-start(f32[192]{0:T(256)} %param.21) | copy-start | bytes 2308
  64.0 144.4 %copy-start.4 = (f32[192]{0:T(256)S(1)}, f32[192]{0:T(256)}, u32[]{:S(2)}) copy-start(f32[192]{0:T(256)} %param.20) | copy-start | bytes 2308
  65.3 6.8 %collective-permute-start = (bf16[15,192]{0,1:T(8,128)(2,1)S(1)}, bf16[15,192]{0,1:T(8,128)(2,1)S(1)}, u32[]{:S(2)}, u32[]{:S(2)}) collective-permute-start(bf16[15,192]{0,1:T(8,128)(2,1)S(1)} %get-tuple-element.13), channel_id=1, source_target_pairs={{0,8},{8,16},{16,24},{24,32},{32,40},{40,48},{48,56},{56,64},{64,7... | collective-permute-start | bytes 17288 | tf_op jit(solution)/shard_map/ppermute | solution.py:16
  69.2 5.4 %collective-permute-start.1 = (bf16[15,192]{0,1:T(8,128)(2,1)S(1)}, bf16[15,192]{0,1:T(8,128)(2,1)S(1)}, u32[]{:S(2)}, u32[]{:S(2)}) collective-permute-start(bf16[15,192]{0,1:T(8,128)(2,1)S(1)} %get-tuple-element.14), channel_id=1, source_target_pairs={{8,0},{16,8},{24,16},{32,24},{40,32},{48,40},{56,48},{64,56},{72,6... | collective-permute-start | bytes 17288 | tf_op jit(solution)/shard_map/ppermute | solution.py:17
  212.3 69.1 %copy-start.1 = (bf16[128,1536]{1,0:T(8,128)(2,1)S(1)}, bf16[128,1536]{1,0:T(8,128)(2,1)}, u32[]{:S(2)}) copy-start(bf16[128,1536]{1,0:T(8,128)(2,1)} %param.13) | copy-start | bytes 1179652
  212.3 70.7 %copy-start.2 = (f32[1536]{0:T(1024)S(1)}, f32[1536]{0:T(1024)}, u32[]{:S(2)}) copy-start(f32[1536]{0:T(1024)} %param.23) | copy-start | bytes 18436
  212.3 72.0 %all-gather.9.cloned.1.call-start = ((), (), s32[]{:S(2)}) async-start(), calls=%async_computation.5 | async-start | bytes 2433024 | tf_op jit(solution)/shard_map/all_gather | solution.py:75
  212.9 96.7 %all-gather.11.cloned.1.call-start = ((), (), s32[]{:S(2)}) async-start(), calls=%async_computation.6 | async-start | bytes 2433024 | tf_op jit(solution)/shard_map/all_gather | solution.py:78
  213.5 141.4 %all-gather.7.cloned.1.call-start = ((), (), s32[]{:S(2)}) async-start(), calls=%async_computation.4 | async-start | bytes 3538944 | tf_op jit(solution)/shard_map/all_gather | solution.py:74
  284.0 157.1 %reduce-scatter.5.cloned.1.call-start = ((), (), s32[]{:S(2)}) async-start(), calls=%async_computation.7 | async-start | bytes 7077888 | tf_op jit(solution)/shard_map/reduce_scatter | solution.py:80
Sparse Core Ops, SparseCore 0:
  12.0 48.5 all-gather.4
  212.5 68.8 reduce-scatter.2
Sparse Core Ops, SparseCore 1:
  215.4 43.3 all-gather.8
  261.1 48.4 all-gather.10
  311.3 43.5 all-gather.6
  367.1 74.1 reduce-scatter.4
where the time goes:
time: 451 us
  waiting for transfers between devices  262 us (58%)
  blocking collectives  127 us (28%)
  matrix products  20.5 us (5%)
  other arithmetic  17.6 us (4%)
  between operations  15.9 us (4%)
  starting transfers between devices  6.2 us (1%)
    reduce_scatter x1, waiting for transfers between devices, shards(): lax.psum_scatter(partial_out, 'tensor', scatter_dimension=0, tiled=True)  74.2 us
    reduce_scatter x1, waiting for transfers between devices, shards(): lax.psum_scatter(jnp.dot(swished, out_weight, preferred_element_type=jnp....  67.8 us
    psum x1, blocking collectives, shards(): lax.psum(jnp.sum(jnp.square(centred) * valid[:, None], axis=0), 'tm')  65.3 us
    psum x1, blocking collectives, shards(): total, count = lax.psum((first_sum, count_local), 'tm')  61.4 us
    all_gather x1, waiting for transfers between devices, shards(): piece = lax.all_gather(normed, 'tensor', axis=0, tiled=True)  45.6 us
    all_gather x1, waiting for transfers between devices, shards(): feed_block = lax.all_gather(feed_normed, 'tensor', axis=0, tiled=True)  45.3 us
    all_gather x1, waiting for transfers between devices, shards(): down_whole = lax.all_gather(down_weight, 'tm', axis=1, tiled=True)  25.3 us
    dot_general x1, matrix products, shards(): jnp.dot(hidden, down_whole, preferred_element_type=jnp.float32)  12.1 us
  transfers between devices with their start and end apart: 8, of which 6 were waited for; matrix products, arithmetic and copies ran while one was open for 1% of the time, Pallas kernels for 0%

commit v1 on v0

--- a/solution.py
+++ b/solution.py
@@ -46,7 +46,8 @@
     positions = lax.axis_index("tm") * block + jnp.arange(block, dtype=jnp.int32)
     valid = ((frame_mask > 0) & (positions < total_length[0])).astype(jnp.float32)
     normed = layer_norm(features, norm_gain).astype(jnp.bfloat16)
-    piece = lax.all_gather(normed, "tensor", axis=0, tiled=True)
+    sent = jnp.stack([normed] * lax.axis_size("tensor"))
+    piece = jnp.concatenate(lax.all_to_all(sent, "tensor", 0, 0), axis=0)
     value = jnp.dot(piece, value_weight, preferred_element_type=jnp.float32)
     gate = jnp.dot(piece, gate_weight, preferred_element_type=jnp.float32)
     glu = (value * jax.nn.sigmoid(gate) * valid[:, None]).astype(jnp.bfloat16)

time: 451 us -> 486 us (1.078)
  waiting for transfers between devices: 262 us -> 288 us
  starting transfers between devices: 6.2 us -> 14.9 us
    all_to_all x0 -> x1, waiting for transfers between devices: none -> 73 us  [shards(): piece = jnp.concatenate(lax.all_to_all(sent, 'tensor', 0, 0), axis=0)]
    all_gather x1 -> x0, waiting for transfers between devices: 45.6 us -> none  [shards(): piece = lax.all_gather(normed, 'tensor', axis=0, tiled=True)]
    all_to_all x0 -> x1, starting transfers between devices: none -> 9.15 us  [shards(): piece = jnp.concatenate(lax.all_to_all(sent, 'tensor', 0, 0), axis=0)]
where the time goes in v1:
time: 486 us
  waiting for transfers between devices  288 us (59%)
  blocking collectives  127 us (26%)
  matrix products  22.2 us (5%)
  other arithmetic  16.1 us (3%)
  between operations  15.8 us (3%)
  starting transfers between devices  14.9 us (3%)
    reduce_scatter x1, waiting for transfers between devices, shards(): lax.psum_scatter(partial_out, 'tensor', scatter_dimension=0, tiled=True)  74.4 us
    all_to_all x1, waiting for transfers between devices, shards(): piece = jnp.concatenate(lax.all_to_all(sent, 'tensor', 0, 0), axis=0)  73 us
    reduce_scatter x1, waiting for transfers between devices, shards(): lax.psum_scatter(jnp.dot(swished, out_weight, preferred_element_type=jnp....  65.2 us
    psum x1, blocking collectives, shards(): lax.psum(jnp.sum(jnp.square(centred) * valid[:, None], axis=0), 'tm')  65.1 us
    psum x1, blocking collectives, shards(): total, count = lax.psum((first_sum, count_local), 'tm')  61.7 us
    all_gather x1, waiting for transfers between devices, shards(): feed_block = lax.all_gather(feed_normed, 'tensor', axis=0, tiled=True)  45.3 us
    all_gather x1, waiting for transfers between devices, shards(): down_whole = lax.all_gather(down_weight, 'tm', axis=1, tiled=True)  25.3 us
    dot_general x1, matrix products, shards(): jnp.dot(hidden, down_whole, preferred_element_type=jnp.float32)  12 us
  transfers between devices with their start and end apart: 8, of which 6 were waited for; matrix products, arithmetic and copies ran while one was open for 1% of the time, Pallas kernels for 0%

profile of v1, /device:TPU:1, one launch (start us, length us, event | category | flops | bytes accessed | tf_op | source)
XLA Modules:
  0.0 485.7 jit_solution(6314348804245181190)
XLA Ops:
  7.4 1.2 convert_reduce_fusion.1
  8.6 1.2 fusion.14
  9.8 1.3 fusion.16
  11.1 1.9 stack.2
  13.1 9.1 %all-to-all-start = ((bf16[8,128,1536]{2,1,0:T(8,128)(2,1)}), bf16[8,128,1536]{2,1,0:T(8,128)(2,1)}, u32[]{:S(2)}, u32[]{:S(2)}) async-start(bf16[8,128,1536]{2,1,0:T(8,128)(2,1)} %stack.2), calls=%async_computation | async-start | bytes 6291456 | tf_op jit(solution)/shard_map/all_to_all | solution.py:50
  23.6 73.0 %all-to-all-done = bf16[8,128,1536]{2,1,0:T(8,128)(2,1)} async-done(((bf16[8,128,1536]{2,1,0:T(8,128)(2,1)}), bf16[8,128,1536]{2,1,0:T(8,128)(2,1)}, u32[]{:S(2)}, u32[]{:S(2)}) %all-to-all-start) | async-done | bytes 3145760 | tf_op jit(solution)/shard_map/all_to_all | solution.py:50
  96.6 3.2 fusion.5
  99.8 3.1 fusion.6
  103.0 3.5 collective-permute-start
  106.5 1.9 collective-permute-start.1
  108.4 3.4 collective-permute-done.1
  111.9 5.6 %multiply_reduce_fusion.1 = (f32[192]{0:T(256)S(1)}, f32[1024,192]{0,1:T(8,128)S(1)}) fusion(f32[1024]{0:T(1024)S(1)} %get-tuple-element.10, f32[192]{0:T(256)S(1)} %bitcast.71, bf16[15,192]{0,1:T(8,128)(2,1)S(1)} %collective-permute-done.1, bf16[1024,192]{0,1:T(8,128)(2,1)S(1)} %fusion.6, f32[192]{0:T(256)S(1)} %bitcast.72, f32[192]{0:T(256)S(1)} %bitcast.43, ...), kind=kLoop, calls=%fused_computation.58 | loop fusion | flops 36175680 | bytes 1219840 | tf_op jit(solution)/shard_map/reduce_sum | solution.py:59
  117.5 61.7 %all-reduce = (f32[192]{0:T(256)S(1)}, f32[]{:T(128)}) all-reduce(f32[192]{0:T(256)S(1)} %get-tuple-element.11, f32[]{:T(128)} %get-tuple-element.9), channel_id=1, replica_groups=mesh['tm'=32,'tensor'=8] {'tm'}, use_global_device_ids=true, to_apply=%region_3.0 | all-reduce | flops 193 | bytes 1544 | tf_op jit(solution)/shard_map/psum | solution.py:60
  180.1 65.1 %psum.23 = f32[192]{0:T(256)S(1)} all-reduce(f32[192]{0:T(256)S(1)} %multiply_reduce_fusion), channel_id=1, replica_groups=mesh['tm'=32,'tensor'=8] {'tm'}, use_global_device_ids=true, to_apply=%region_7.0 | all-reduce | flops 192 | bytes 1536 | tf_op jit(solution)/shard_map/psum | solution.py:63
  245.2 0.7 add_rsqrt_fusion
  245.9 3.9 fusion.19
  251.0 65.2 %reduce-scatter.3.cloned.1.call-done = f32[128,1536]{1,0:T(8,128)} async-done(((f32[1024,1536]{1,0:T(8,128)}), f32[128,1536]{1,0:T(8,128)}) %reduce-scatter.3.cloned.1.call-update) | async-done | bytes 786448 | tf_op jit(solution)/shard_map/reduce_scatter | solution.py:67
  316.2 1.3 convert_reduce_fusion
  317.8 1.0 fusion.13
  319.1 25.3 %all-gather.8.cloned.1.call-done = bf16[768,1536]{0,1:T(8,128)(2,1)} async-done(((bf16[768,48]{0,1:T(8,128)(2,1)}), bf16[768,1536]{0,1:T(8,128)(2,1)}) %all-gather.8.cloned.1.call-update) | async-done | bytes 2359312 | tf_op jit(solution)/shard_map/all_gather | solution.py:79
  344.4 45.3 %all-gather.4.cloned.1.call-done = bf16[1024,1536]{1,0:T(8,128)(2,1)} async-done(((bf16[128,1536]{1,0:T(8,128)(2,1)}), bf16[1024,1536]{1,0:T(8,128)(2,1)}) %all-gather.4.cloned.1.call-update) | async-done | bytes 3145744 | tf_op jit(solution)/shard_map/all_gather | solution.py:75
  389.7 12.0 %fusion = f32[1024,1536]{1,0:T(8,128)} fusion(bf16[768,1536]{0,1:T(8,128)(2,1)} %all-gather.8.cloned.1.call-done, bf16[1024,1536]{1,0:T(8,128)(2,1)} %all-gather.4.cloned.1.call-done, bf16[1536,768]{1,0:T(8,128)(2,1)} %all-gather.6.cloned.1.call-done), kind=kOutput, calls=%fused_computation.29 | convolution fusion | flops 4835770368 | bytes 14155776 | tf_op jit(solution)/shard_map/dot_general | solution.py:80
  401.8 74.4 %reduce-scatter.5.cloned.1.call-done = f32[128,1536]{1,0:T(8,128)} async-done(((f32[1024,1536]{1,0:T(8,128)}), f32[128,1536]{1,0:T(8,128)}) %reduce-scatter.5.cloned.1.call-update) | async-done | bytes 786448 | tf_op jit(solution)/shard_map/reduce_scatter | solution.py:81
  476.2 2.0 fusion.18
  (41 shorter events, 3.5 us)
Async XLA Ops:
  7.4 238.5 %copy-start = (bf16[192,1536]{1,0:T(8,128)(2,1)S(1)}, bf16[192,1536]{1,0:T(8,128)(2,1)}, u32[]{:S(2)}) copy-start(bf16[192,1536]{1,0:T(8,128)(2,1)} %param.22) | copy-start | bytes 1769476
  13.1 9.9 %copy-start.4 = (s32[1024]{0:T(1024)S(1)}, s32[1024]{0:T(1024)}, u32[]{:S(2)}) copy-start(s32[1024]{0:T(1024)} %param.14) | copy-start | bytes 12292
  13.1 10.5 %copy-start.2 = (f32[31,192]{1,0:T(8,128)S(1)}, f32[31,192]{1,0:T(8,128)}, u32[]{:S(2)}) copy-start(f32[31,192]{1,0:T(8,128)} %param.19) | copy-start | bytes 71428
  13.1 83.5 %copy-start.7 = (bf16[1536,192]{0,1:T(8,128)(2,1)S(1)}, bf16[1536,192]{0,1:T(8,128)(2,1)}, u32[]{:S(2)}) copy-start(bf16[1536,192]{0,1:T(8,128)(2,1)} %param.18) | copy-start | bytes 1769476
  13.1 83.5 %all-to-all-start = ((bf16[8,128,1536]{2,1,0:T(8,128)(2,1)}), bf16[8,128,1536]{2,1,0:T(8,128)(2,1)}, u32[]{:S(2)}, u32[]{:S(2)}) async-start(bf16[8,128,1536]{2,1,0:T(8,128)(2,1)} %stack.2), calls=%async_computation | async-start | bytes 6291456 | tf_op jit(solution)/shard_map/all_to_all | solution.py:50
  22.2 294.0 %reduce-scatter.3.cloned.1.call-start = ((), (), s32[]{:S(2)}) async-start(), calls=%async_computation.3 | async-start | bytes 7077888 | tf_op jit(solution)/shard_map/reduce_scatter | solution.py:67
  96.6 3.2 copy-start.8
  99.8 146.1 %copy-start.5 = (f32[192]{0:T(256)S(1)}, f32[192]{0:T(256)}, u32[]{:S(2)}) copy-start(f32[192]{0:T(256)} %param.21) | copy-start | bytes 2308
  99.8 146.1 %copy-start.6 = (f32[192]{0:T(256)S(1)}, f32[192]{0:T(256)}, u32[]{:S(2)}) copy-start(f32[192]{0:T(256)} %param.20) | copy-start | bytes 2308
  103.0 5.5 %collective-permute-start = (bf16[15,192]{0,1:T(8,128)(2,1)S(1)}, bf16[15,192]{0,1:T(8,128)(2,1)S(1)}, u32[]{:S(2)}, u32[]{:S(2)}) collective-permute-start(bf16[15,192]{0,1:T(8,128)(2,1)S(1)} %get-tuple-element.13), channel_id=1, source_target_pairs={{0,8},{8,16},{16,24},{24,32},{32,40},{40,48},{48,56},{56,64},{64,7... | collective-permute-start | bytes 17288 | tf_op jit(solution)/shard_map/ppermute | solution.py:16
  106.5 5.4 %collective-permute-start.1 = (bf16[15,192]{0,1:T(8,128)(2,1)S(1)}, bf16[15,192]{0,1:T(8,128)(2,1)S(1)}, u32[]{:S(2)}, u32[]{:S(2)}) collective-permute-start(bf16[15,192]{0,1:T(8,128)(2,1)S(1)} %get-tuple-element.14), channel_id=1, source_target_pairs={{8,0},{16,8},{24,16},{32,24},{40,32},{48,40},{56,48},{64,56},{72,6... | collective-permute-start | bytes 17288 | tf_op jit(solution)/shard_map/ppermute | solution.py:17
  249.7 66.5 %copy-start.1 = (bf16[128,1536]{1,0:T(8,128)(2,1)S(1)}, bf16[128,1536]{1,0:T(8,128)(2,1)}, u32[]{:S(2)}) copy-start(bf16[128,1536]{1,0:T(8,128)(2,1)} %param.13) | copy-start | bytes 1179652
  249.7 68.1 %copy-start.3 = (f32[1536]{0:T(1024)S(1)}, f32[1536]{0:T(1024)}, u32[]{:S(2)}) copy-start(f32[1536]{0:T(1024)} %param.23) | copy-start | bytes 18436
  249.8 69.3 %all-gather.6.cloned.1.call-start = ((), (), s32[]{:S(2)}) async-start(), calls=%async_computation.5 | async-start | bytes 2433024 | tf_op jit(solution)/shard_map/all_gather | solution.py:76
  250.3 94.1 %all-gather.8.cloned.1.call-start = ((), (), s32[]{:S(2)}) async-start(), calls=%async_computation.6 | async-start | bytes 2433024 | tf_op jit(solution)/shard_map/all_gather | solution.py:79
  250.9 138.8 %all-gather.4.cloned.1.call-start = ((), (), s32[]{:S(2)}) async-start(), calls=%async_computation.4 | async-start | bytes 3538944 | tf_op jit(solution)/shard_map/all_gather | solution.py:75
  318.9 157.3 %reduce-scatter.5.cloned.1.call-start = ((), (), s32[]{:S(2)}) async-start(), calls=%async_computation.7 | async-start | bytes 7077888 | tf_op jit(solution)/shard_map/reduce_scatter | solution.py:81
Sparse Core Ops, SparseCore 0:
  249.9 66.2 reduce-scatter.2
  401.9 74.2 reduce-scatter.4
Sparse Core Ops, SparseCore 1:
  252.8 40.7 all-gather.5
  295.9 48.4 all-gather.7
  346.1 43.5 all-gather.3
